TPU v7x, 128 devices: a whole 4x4x4 slice. The times are simulated.
128 devices in a mesh: gx: 8 (over z, core), gy: 16 (over y, x).
Axes of the slice: x: 4, y: 4, z: 4, core: 2. Of those that a mesh axis runs over, the one named last changes fastest.
Arguments:
- hidden_in: bfloat16 [32768, 3584], P(('gx', 'gy')), may hold values from -6 to 6
- lengths: int32 [8, 4], P('gx'), may hold values from 1 to 2048, 4096 in all within a row
- attn_norm: float32 [3584], replicated, may hold values from 0.5 to 1.5
- qkv_weight: bfloat16 [3584, 4608], P('gx', 'gy'), may hold values from -0.09375 to 0.09375
- qkv_bias: float32 [4608], replicated, may hold values from -5 to 5
Outputs:
- attn: bfloat16 [32768, 3584], P(('gx', 'gy'))
- kv_rows: bfloat16 [32768, 1024], P(('gx', 'gy'))
Inputs may be any that keep to these rules, and one draw needn't show every extreme that they name: Each row of lengths sums to 4096; the longest of each row is exactly 2048.
All inputs are finite; a program needn't handle non-finite values.
Results may differ from a plain program's by a relative error of at most 0.0035.
The roundings to bfloat16 on the way count: a program that leaves them out, or rounds other values in their place, can miss the bound.
Values may be sent and summed in bfloat16 or wider, within the bound.
No kernel may reach another device: no remote copies, remote signals or barrier semaphores. Data moves between devices by JAX's collectives and lax.ppermute only.
A program may use at most 128 MiB of HBM per device.

v0:
```python
import math
import jax
import jax.numpy as jnp
from jax import lax
from jax.sharding import PartitionSpec as P

HEADS = 28
KV_HEADS = 4
HEAD_DIM = 128
key_span = 512


def norm_rows(values, gain):
    wide = values.astype(jnp.float32)
    scale = lax.rsqrt(jnp.mean(wide * wide, axis=1, keepdims=True) + 1e-06)
    return (wide * scale * gain[None, :]).astype(jnp.bfloat16)


def segment_of(index, ends):
    return jnp.sum((ends[None, :] <= index[:, None]).astype(jnp.int32), axis=1)


def rotate(block, pos, heads):
    half = HEAD_DIM // 2
    freqs = 1000000.0 ** (-2.0 * jnp.arange(half, dtype=jnp.float32) / HEAD_DIM)
    angle = pos.astype(jnp.float32)[:, None, None] * freqs[None, None, :]
    wide = block.astype(jnp.float32).reshape(block.shape[0], heads, HEAD_DIM)
    first, second = (wide[..., :half], wide[..., half:])
    turned = jnp.concatenate(
        [
            first * jnp.cos(angle) - second * jnp.sin(angle),
            second * jnp.cos(angle) + first * jnp.sin(angle),
        ],
        axis=2,
    )
    return turned.reshape(block.shape[0], heads * HEAD_DIM).astype(jnp.bfloat16)


def project_joined(normed, weight, bias):
    grouped = lax.all_gather(normed, "gy", axis=0, tiled=True)
    summed = jnp.dot(
        grouped,
        lax.all_gather(weight, "gx", axis=0, tiled=True),
        preferred_element_type=jnp.float32,
    )
    width = weight.shape[1]
    bias_block = lax.dynamic_slice_in_dim(bias, lax.axis_index("gy") * width, width, 0)
    block_out = (summed + bias_block[None, :]).astype(jnp.bfloat16)
    return lax.all_to_all(block_out, "gy", split_axis=0, concat_axis=1, tiled=True)


def on_device(hidden_in, lengths, attn_norm, qkv_weight, qkv_bias):
    rows = hidden_in.shape[0]
    first = lax.axis_index("gy") * rows
    row_lengths = lengths[0]
    qdim = HEADS * HEAD_DIM
    kdim = KV_HEADS * HEAD_DIM
    group = HEADS // KV_HEADS
    normed = norm_rows(hidden_in, attn_norm)
    joined = project_joined(normed, qkv_weight, qkv_bias)
    ends = jnp.cumsum(row_lengths)
    tokens_here = first + jnp.arange(rows, dtype=jnp.int32)
    before = ends[None, :] <= tokens_here[:, None]
    seg_here = jnp.sum(before.astype(jnp.int32), axis=1)
    begin = jnp.sum(jnp.where(before, row_lengths[None, :], 0), axis=1)
    pos = tokens_here - begin
    queries = rotate(joined[:, :qdim], pos, HEADS).reshape(rows, KV_HEADS, group, HEAD_DIM)
    keys = rotate(joined[:, qdim : qdim + kdim], pos, KV_HEADS)
    kv_rows = jnp.concatenate([keys, joined[:, qdim + kdim :]], axis=1)
    scale = 1.0 / HEAD_DIM**0.5

    def attend(carry, piece, start):
        running, total, summed = carry
        key_count = piece.shape[0]
        key_index = start + jnp.arange(key_count, dtype=jnp.int32)
        key_seg = segment_of(key_index, ends)
        key_part = piece[:, :kdim].reshape(key_count, KV_HEADS, HEAD_DIM)
        value_part = piece[:, kdim:].reshape(key_count, KV_HEADS, HEAD_DIM)
        scores = (
            jnp.einsum("rgho,ngo->ghrn", queries, key_part, preferred_element_type=jnp.float32)
            * scale
        )
        allowed = (seg_here[:, None] == key_seg[None, :]) & (
            key_index[None, :] <= tokens_here[:, None]
        )
        newest = jnp.maximum(running, jnp.max(jnp.where(allowed, scores, -1e30), axis=3))
        shrink = jnp.exp(running - newest)
        weights = jnp.where(allowed, jnp.exp(scores - newest[..., None]), 0.0)
        total = total * shrink + jnp.sum(weights, axis=3)
        summed = summed * shrink[..., None] + jnp.einsum(
            "ghrn,ngo->ghro",
            weights.astype(jnp.bfloat16),
            value_part,
            preferred_element_type=jnp.float32,
        )
        return (newest, total, summed)

    def visit(carry, piece, start):
        return attend(carry, piece, start)

    start_state = (
        jnp.full((KV_HEADS, group, rows), -1e30, jnp.float32),
        jnp.zeros((KV_HEADS, group, rows), jnp.float32),
        jnp.zeros((KV_HEADS, group, rows, HEAD_DIM), jnp.float32),
    )
    piece = lax.all_gather(kv_rows, "gy", axis=0, tiled=True)
    length = piece.shape[0]
    span = math.gcd(length, key_span)
    stacked = piece.reshape(length // span, span, piece.shape[1])
    offsets = jnp.arange(length // span, dtype=jnp.int32) * span

    def advance(state, item):
        return (visit(state, item[0], item[1]), None)

    final_state, unused = lax.scan(advance, start_state, (stacked, offsets))
    running, total, summed = final_state
    attn = (
        jnp.transpose(summed / total[..., None], (2, 0, 1, 3))
        .reshape(rows, qdim)
        .astype(jnp.bfloat16)
    )
    return (attn, kv_rows)


def solution(mesh):
    placed = (P(("gx", "gy"), None), P("gx", None), P(), P("gx", "gy"), P())
    return jax.shard_map(
        on_device,
        mesh=mesh,
        in_specs=placed,
        out_specs=(P(("gx", "gy"), None), P(("gx", "gy"), None)),
        check_vma=False,
    )
```

profile of v0, /device:TPU:0, one launch (start us, length us, event | category | flops | bytes accessed | tf_op | source)
XLA Modules:
  0.0 595.3 jit_solution(592481126304964280)
XLA Ops:
  13.9 24.0 %all-gather.9.cloned.1.call-done = bf16[8,448,288]{1,2,0:T(8,128)(2,1)} async-done(((bf16[1,448,288]{1,2,0:T(8,128)(2,1)}), bf16[8,448,288]{1,2,0:T(8,128)(2,1)}) %all-gather.9.cloned.1.call-update) | async-done | bytes 2064400 | tf_op jit(solution)/shard_map/all_gather | solution.py:43
  44.5 172.0 %all-gather.5.cloned.1.call-done = bf16[4096,3584]{1,0:T(8,128)(2,1)} async-done(((bf16[256,3584]{1,0:T(8,128)(2,1)}), bf16[4096,3584]{1,0:T(8,128)(2,1)}) %all-gather.5.cloned.1.call-update) | async-done | bytes 29360144 | tf_op jit(solution)/shard_map/all_gather | solution.py:40
  216.6 14.7 %fusion.16 = bf16[4096,288]{0,1:T(8,128)(2,1)S(1)} fusion(bf16[4096,3584]{1,0:T(8,128)(2,1)} %all-gather.5.cloned.1.call-done, bf16[3584,288]{0,1:T(8,128)(2,1)} %reshape.172, f32[288]{0:T(512)S(1)} %dynamic_slice.11), kind=kOutput, calls=%fused_computation.25 | convolution fusion | flops 8458076160 | bytes 33784960 | tf_op jit(solution)/shard_map/dot_general | solution.py:41
  233.0 5.3 all-to-all-start
  239.1 34.4 %all-to-all-done = bf16[16,256,288]{1,2,0:T(8,128)(2,1)S(1)} async-done(((bf16[16,256,288]{1,2,0:T(8,128)(2,1)}), bf16[16,256,288]{1,2,0:T(8,128)(2,1)S(1)}, u32[]{:S(2)}, u32[]{:S(2)}) %all-to-all-start) | async-done | bytes 2359328 | tf_op jit(solution)/shard_map/all_to_all | solution.py:49
  283.8 65.9 %all-gather.7.cloned.1.call-done = bf16[4096,1024]{0,1:T(8,128)(2,1)} async-done(((bf16[256,1024]{0,1:T(8,128)(2,1)}), bf16[4096,1024]{0,1:T(8,128)(2,1)}) %all-gather.7.cloned.1.call-update) | async-done | bytes 8388624 | tf_op jit(solution)/shard_map/all_gather | solution.py:106
  349.7 7.5 %copy.52 = bf16[128,8,8,512]{3,2,0,1:T(8,128)(2,1)} copy(bf16[128,8,8,512]{3,2,1,0:T(8,128)(2,1)} %bitcast.86) | data formatting | bytes 16777216 | tf_op jit(solution)/shard_map/reshape | solution.py:109
  357.2 222.0 %while.15 = (s32[]{:T(128)}, f32[4,7,256]{2,1,0:T(8,128)S(1)}, f32[4,7,256]{2,1,0:T(8,128)S(1)}, f32[4,7,256,128]{3,2,1,0:T(8,128)}, s32[256]{0:T(256)S(1)}, /*i...) while((s32[]{:T(128)}, f32[4,7,256]{2,1,0:T(8,128)S(1)}, ...), condition=%wide.region_8.9_spmd.clone, body=%wide.region_4.8_spmd.clone.sunk | while | flops 1922606336 | bytes 88814816 | solution.py:115
  360.1 6.5 %fusion.43 = (f32[4,7,256]{2,1,0:T(8,128)S(1)}, f32[4,512,256,7]{2,1,3,0:T(8,128)}) fusion(pred[256,512]{0,1:T(8,128)(4,1)S(1)} %compare_and_fusion.2, bf16[512,4,128,1]{0,2,3,1:T(8,128)(2,1)S(1)} %bitcast.80, bf16[256,4,7,128]{3,0,2,1:T(8,128)(2,1)S(1)} %get-tuple-element.270), kind=kOutput, calls=%fused_computation.3.clone.1 | convolution fusion | flops 950526976 | bytes 17199104 | tf_op jit(solution)/shard_map/while/body/eval_jaxpr/rgho,ngo->ghrn/dot_general | solution.py:80
  366.6 8.3 %fusion.44 = f32[4,7,256]{2,1,0:T(8,128)S(1)} fusion(f32[4,512,256,7]{2,1,3,0:T(8,128)} %get-tuple-element.234, f32[4,7,256]{2,1,0:T(8,128)S(1)} %select_maximum_fusion.2, pred[256,512]{0,1:T(8,128)(4,1)S(1)} %compare_and_fusion.2), kind=kLoop, calls=%fused_computation.7.clone.1 | loop fusion | flops 14672896 | bytes 14868480 | tf_op jit(solution)/shard_map/while/body/eval_jaxpr/reduce_sum | solution.py:89
  375.0 8.0 %fusion.46 = f32[4,7,256,128]{3,2,1,0:T(8,128)S(1)} fusion(f32[4,7,256,128]{3,2,1,0:T(8,128)S(1)} %copy-done.1, bf16[512,4,128,1]{0,2,3,1:T(8,128)(2,1)S(1)} %bitcast.82, f32[4,512,256,7]{2,1,3,0:T(8,128)} %get-tuple-element.234, f32[4,7,256]{2,1,0:T(8,128)S(1)} %select_maximum_fusion.2, pred[256,512]{0,1:T(8,128)(4,1)S(1)} %compare_and_fusion.2, ...), kind=kOutput, calls=%fused_computation.11.clone.1 | convolution fusion | flops 956956672 | bytes 22732800 | tf_op jit(solution)/shard_map/while/body/eval_jaxpr/ghrn,ngo->ghro/dot_general | solution.py:90
  387.8 6.5 %fusion.43 = (f32[4,7,256]{2,1,0:T(8,128)S(1)}, f32[4,512,256,7]{2,1,3,0:T(8,128)}) fusion(pred[256,512]{0,1:T(8,128)(4,1)S(1)} %compare_and_fusion.2, bf16[512,4,128,1]{0,2,3,1:T(8,128)(2,1)S(1)} %bitcast.80, bf16[256,4,7,128]{3,0,2,1:T(8,128)(2,1)S(1)} %get-tuple-element.270), kind=kOutput, calls=%fused_computation.3.clone.1 | convolution fusion | flops 950526976 | bytes 17199104 | tf_op jit(solution)/shard_map/while/body/eval_jaxpr/rgho,ngo->ghrn/dot_general | solution.py:80
  394.4 8.3 %fusion.44 = f32[4,7,256]{2,1,0:T(8,128)S(1)} fusion(f32[4,512,256,7]{2,1,3,0:T(8,128)} %get-tuple-element.234, f32[4,7,256]{2,1,0:T(8,128)S(1)} %select_maximum_fusion.2, pred[256,512]{0,1:T(8,128)(4,1)S(1)} %compare_and_fusion.2), kind=kLoop, calls=%fused_computation.7.clone.1 | loop fusion | flops 14672896 | bytes 14868480 | tf_op jit(solution)/shard_map/while/body/eval_jaxpr/reduce_sum | solution.py:89
  402.7 8.0 %fusion.46 = f32[4,7,256,128]{3,2,1,0:T(8,128)S(1)} fusion(f32[4,7,256,128]{3,2,1,0:T(8,128)S(1)} %copy-done.1, bf16[512,4,128,1]{0,2,3,1:T(8,128)(2,1)S(1)} %bitcast.82, f32[4,512,256,7]{2,1,3,0:T(8,128)} %get-tuple-element.234, f32[4,7,256]{2,1,0:T(8,128)S(1)} %select_maximum_fusion.2, pred[256,512]{0,1:T(8,128)(4,1)S(1)} %compare_and_fusion.2, ...), kind=kOutput, calls=%fused_computation.11.clone.1 | convolution fusion | flops 956956672 | bytes 22732800 | tf_op jit(solution)/shard_map/while/body/eval_jaxpr/ghrn,ngo->ghro/dot_general | solution.py:90
  415.6 6.5 %fusion.43 = (f32[4,7,256]{2,1,0:T(8,128)S(1)}, f32[4,512,256,7]{2,1,3,0:T(8,128)}) fusion(pred[256,512]{0,1:T(8,128)(4,1)S(1)} %compare_and_fusion.2, bf16[512,4,128,1]{0,2,3,1:T(8,128)(2,1)S(1)} %bitcast.80, bf16[256,4,7,128]{3,0,2,1:T(8,128)(2,1)S(1)} %get-tuple-element.270), kind=kOutput, calls=%fused_computation.3.clone.1 | convolution fusion | flops 950526976 | bytes 17199104 | tf_op jit(solution)/shard_map/while/body/eval_jaxpr/rgho,ngo->ghrn/dot_general | solution.py:80
  422.1 8.3 %fusion.44 = f32[4,7,256]{2,1,0:T(8,128)S(1)} fusion(f32[4,512,256,7]{2,1,3,0:T(8,128)} %get-tuple-element.234, f32[4,7,256]{2,1,0:T(8,128)S(1)} %select_maximum_fusion.2, pred[256,512]{0,1:T(8,128)(4,1)S(1)} %compare_and_fusion.2), kind=kLoop, calls=%fused_computation.7.clone.1 | loop fusion | flops 14672896 | bytes 14868480 | tf_op jit(solution)/shard_map/while/body/eval_jaxpr/reduce_sum | solution.py:89
  430.5 8.0 %fusion.46 = f32[4,7,256,128]{3,2,1,0:T(8,128)S(1)} fusion(f32[4,7,256,128]{3,2,1,0:T(8,128)S(1)} %copy-done.1, bf16[512,4,128,1]{0,2,3,1:T(8,128)(2,1)S(1)} %bitcast.82, f32[4,512,256,7]{2,1,3,0:T(8,128)} %get-tuple-element.234, f32[4,7,256]{2,1,0:T(8,128)S(1)} %select_maximum_fusion.2, pred[256,512]{0,1:T(8,128)(4,1)S(1)} %compare_and_fusion.2, ...), kind=kOutput, calls=%fused_computation.11.clone.1 | convolution fusion | flops 956956672 | bytes 22732800 | tf_op jit(solution)/shard_map/while/body/eval_jaxpr/ghrn,ngo->ghro/dot_general | solution.py:90
  443.3 6.5 %fusion.43 = (f32[4,7,256]{2,1,0:T(8,128)S(1)}, f32[4,512,256,7]{2,1,3,0:T(8,128)}) fusion(pred[256,512]{0,1:T(8,128)(4,1)S(1)} %compare_and_fusion.2, bf16[512,4,128,1]{0,2,3,1:T(8,128)(2,1)S(1)} %bitcast.80, bf16[256,4,7,128]{3,0,2,1:T(8,128)(2,1)S(1)} %get-tuple-element.270), kind=kOutput, calls=%fused_computation.3.clone.1 | convolution fusion | flops 950526976 | bytes 17199104 | tf_op jit(solution)/shard_map/while/body/eval_jaxpr/rgho,ngo->ghrn/dot_general | solution.py:80
  449.9 8.3 %fusion.44 = f32[4,7,256]{2,1,0:T(8,128)S(1)} fusion(f32[4,512,256,7]{2,1,3,0:T(8,128)} %get-tuple-element.234, f32[4,7,256]{2,1,0:T(8,128)S(1)} %select_maximum_fusion.2, pred[256,512]{0,1:T(8,128)(4,1)S(1)} %compare_and_fusion.2), kind=kLoop, calls=%fused_computation.7.clone.1 | loop fusion | flops 14672896 | bytes 14868480 | tf_op jit(solution)/shard_map/while/body/eval_jaxpr/reduce_sum | solution.py:89
  458.2 8.0 %fusion.46 = f32[4,7,256,128]{3,2,1,0:T(8,128)S(1)} fusion(f32[4,7,256,128]{3,2,1,0:T(8,128)S(1)} %copy-done.1, bf16[512,4,128,1]{0,2,3,1:T(8,128)(2,1)S(1)} %bitcast.82, f32[4,512,256,7]{2,1,3,0:T(8,128)} %get-tuple-element.234, f32[4,7,256]{2,1,0:T(8,128)S(1)} %select_maximum_fusion.2, pred[256,512]{0,1:T(8,128)(4,1)S(1)} %compare_and_fusion.2, ...), kind=kOutput, calls=%fused_computation.11.clone.1 | convolution fusion | flops 956956672 | bytes 22732800 | tf_op jit(solution)/shard_map/while/body/eval_jaxpr/ghrn,ngo->ghro/dot_general | solution.py:90
  471.1 6.5 %fusion.43 = (f32[4,7,256]{2,1,0:T(8,128)S(1)}, f32[4,512,256,7]{2,1,3,0:T(8,128)}) fusion(pred[256,512]{0,1:T(8,128)(4,1)S(1)} %compare_and_fusion.2, bf16[512,4,128,1]{0,2,3,1:T(8,128)(2,1)S(1)} %bitcast.80, bf16[256,4,7,128]{3,0,2,1:T(8,128)(2,1)S(1)} %get-tuple-element.270), kind=kOutput, calls=%fused_computation.3.clone.1 | convolution fusion | flops 950526976 | bytes 17199104 | tf_op jit(solution)/shard_map/while/body/eval_jaxpr/rgho,ngo->ghrn/dot_general | solution.py:80
  477.6 8.3 %fusion.44 = f32[4,7,256]{2,1,0:T(8,128)S(1)} fusion(f32[4,512,256,7]{2,1,3,0:T(8,128)} %get-tuple-element.234, f32[4,7,256]{2,1,0:T(8,128)S(1)} %select_maximum_fusion.2, pred[256,512]{0,1:T(8,128)(4,1)S(1)} %compare_and_fusion.2), kind=kLoop, calls=%fused_computation.7.clone.1 | loop fusion | flops 14672896 | bytes 14868480 | tf_op jit(solution)/shard_map/while/body/eval_jaxpr/reduce_sum | solution.py:89
  486.0 8.0 %fusion.46 = f32[4,7,256,128]{3,2,1,0:T(8,128)S(1)} fusion(f32[4,7,256,128]{3,2,1,0:T(8,128)S(1)} %copy-done.1, bf16[512,4,128,1]{0,2,3,1:T(8,128)(2,1)S(1)} %bitcast.82, f32[4,512,256,7]{2,1,3,0:T(8,128)} %get-tuple-element.234, f32[4,7,256]{2,1,0:T(8,128)S(1)} %select_maximum_fusion.2, pred[256,512]{0,1:T(8,128)(4,1)S(1)} %compare_and_fusion.2, ...), kind=kOutput, calls=%fused_computation.11.clone.1 | convolution fusion | flops 956956672 | bytes 22732800 | tf_op jit(solution)/shard_map/while/body/eval_jaxpr/ghrn,ngo->ghro/dot_general | solution.py:90
  498.8 6.5 %fusion.43 = (f32[4,7,256]{2,1,0:T(8,128)S(1)}, f32[4,512,256,7]{2,1,3,0:T(8,128)}) fusion(pred[256,512]{0,1:T(8,128)(4,1)S(1)} %compare_and_fusion.2, bf16[512,4,128,1]{0,2,3,1:T(8,128)(2,1)S(1)} %bitcast.80, bf16[256,4,7,128]{3,0,2,1:T(8,128)(2,1)S(1)} %get-tuple-element.270), kind=kOutput, calls=%fused_computation.3.clone.1 | convolution fusion | flops 950526976 | bytes 17199104 | tf_op jit(solution)/shard_map/while/body/eval_jaxpr/rgho,ngo->ghrn/dot_general | solution.py:80
  505.4 8.3 %fusion.44 = f32[4,7,256]{2,1,0:T(8,128)S(1)} fusion(f32[4,512,256,7]{2,1,3,0:T(8,128)} %get-tuple-element.234, f32[4,7,256]{2,1,0:T(8,128)S(1)} %select_maximum_fusion.2, pred[256,512]{0,1:T(8,128)(4,1)S(1)} %compare_and_fusion.2), kind=kLoop, calls=%fused_computation.7.clone.1 | loop fusion | flops 14672896 | bytes 14868480 | tf_op jit(solution)/shard_map/while/body/eval_jaxpr/reduce_sum | solution.py:89
  513.7 8.0 %fusion.46 = f32[4,7,256,128]{3,2,1,0:T(8,128)S(1)} fusion(f32[4,7,256,128]{3,2,1,0:T(8,128)S(1)} %copy-done.1, bf16[512,4,128,1]{0,2,3,1:T(8,128)(2,1)S(1)} %bitcast.82, f32[4,512,256,7]{2,1,3,0:T(8,128)} %get-tuple-element.234, f32[4,7,256]{2,1,0:T(8,128)S(1)} %select_maximum_fusion.2, pred[256,512]{0,1:T(8,128)(4,1)S(1)} %compare_and_fusion.2, ...), kind=kOutput, calls=%fused_computation.11.clone.1 | convolution fusion | flops 956956672 | bytes 22732800 | tf_op jit(solution)/shard_map/while/body/eval_jaxpr/ghrn,ngo->ghro/dot_general | solution.py:90
  526.6 6.5 %fusion.43 = (f32[4,7,256]{2,1,0:T(8,128)S(1)}, f32[4,512,256,7]{2,1,3,0:T(8,128)}) fusion(pred[256,512]{0,1:T(8,128)(4,1)S(1)} %compare_and_fusion.2, bf16[512,4,128,1]{0,2,3,1:T(8,128)(2,1)S(1)} %bitcast.80, bf16[256,4,7,128]{3,0,2,1:T(8,128)(2,1)S(1)} %get-tuple-element.270), kind=kOutput, calls=%fused_computation.3.clone.1 | convolution fusion | flops 950526976 | bytes 17199104 | tf_op jit(solution)/shard_map/while/body/eval_jaxpr/rgho,ngo->ghrn/dot_general | solution.py:80
  533.1 8.3 %fusion.44 = f32[4,7,256]{2,1,0:T(8,128)S(1)} fusion(f32[4,512,256,7]{2,1,3,0:T(8,128)} %get-tuple-element.234, f32[4,7,256]{2,1,0:T(8,128)S(1)} %select_maximum_fusion.2, pred[256,512]{0,1:T(8,128)(4,1)S(1)} %compare_and_fusion.2), kind=kLoop, calls=%fused_computation.7.clone.1 | loop fusion | flops 14672896 | bytes 14868480 | tf_op jit(solution)/shard_map/while/body/eval_jaxpr/reduce_sum | solution.py:89
  541.5 8.0 %fusion.46 = f32[4,7,256,128]{3,2,1,0:T(8,128)S(1)} fusion(f32[4,7,256,128]{3,2,1,0:T(8,128)S(1)} %copy-done.1, bf16[512,4,128,1]{0,2,3,1:T(8,128)(2,1)S(1)} %bitcast.82, f32[4,512,256,7]{2,1,3,0:T(8,128)} %get-tuple-element.234, f32[4,7,256]{2,1,0:T(8,128)S(1)} %select_maximum_fusion.2, pred[256,512]{0,1:T(8,128)(4,1)S(1)} %compare_and_fusion.2, ...), kind=kOutput, calls=%fused_computation.11.clone.1 | convolution fusion | flops 956956672 | bytes 22732800 | tf_op jit(solution)/shard_map/while/body/eval_jaxpr/ghrn,ngo->ghro/dot_general | solution.py:90
  554.3 6.5 %fusion.43 = (f32[4,7,256]{2,1,0:T(8,128)S(1)}, f32[4,512,256,7]{2,1,3,0:T(8,128)}) fusion(pred[256,512]{0,1:T(8,128)(4,1)S(1)} %compare_and_fusion.2, bf16[512,4,128,1]{0,2,3,1:T(8,128)(2,1)S(1)} %bitcast.80, bf16[256,4,7,128]{3,0,2,1:T(8,128)(2,1)S(1)} %get-tuple-element.270), kind=kOutput, calls=%fused_computation.3.clone.1 | convolution fusion | flops 950526976 | bytes 17199104 | tf_op jit(solution)/shard_map/while/body/eval_jaxpr/rgho,ngo->ghrn/dot_general | solution.py:80
  560.9 8.3 %fusion.44 = f32[4,7,256]{2,1,0:T(8,128)S(1)} fusion(f32[4,512,256,7]{2,1,3,0:T(8,128)} %get-tuple-element.234, f32[4,7,256]{2,1,0:T(8,128)S(1)} %select_maximum_fusion.2, pred[256,512]{0,1:T(8,128)(4,1)S(1)} %compare_and_fusion.2), kind=kLoop, calls=%fused_computation.7.clone.1 | loop fusion | flops 14672896 | bytes 14868480 | tf_op jit(solution)/shard_map/while/body/eval_jaxpr/reduce_sum | solution.py:89
  569.2 8.0 %fusion.46 = f32[4,7,256,128]{3,2,1,0:T(8,128)S(1)} fusion(f32[4,7,256,128]{3,2,1,0:T(8,128)S(1)} %copy-done.1, bf16[512,4,128,1]{0,2,3,1:T(8,128)(2,1)S(1)} %bitcast.82, f32[4,512,256,7]{2,1,3,0:T(8,128)} %get-tuple-element.234, f32[4,7,256]{2,1,0:T(8,128)S(1)} %select_maximum_fusion.2, pred[256,512]{0,1:T(8,128)(4,1)S(1)} %compare_and_fusion.2, ...), kind=kOutput, calls=%fused_computation.11.clone.1 | convolution fusion | flops 956956672 | bytes 22732800 | tf_op jit(solution)/shard_map/while/body/eval_jaxpr/ghrn,ngo->ghro/dot_general | solution.py:90
  (153 shorter events, 74.2 us)
Async XLA Ops:
  7.2 30.8 %all-gather.9.cloned.1.call-start = ((), (), s32[]{:S(2)}) async-start(), calls=%async_computation.3 | async-start | bytes 2654208 | tf_op jit(solution)/shard_map/all_gather | solution.py:43
  7.9 208.7 %all-gather.5.cloned.1.call-start = ((), (), s32[]{:S(2)}) async-start(), calls=%async_computation.1 | async-start | bytes 31195136 | tf_op jit(solution)/shard_map/all_gather | solution.py:40
  231.3 7.2 %copy-start.3 = (s32[1,4]{1,0:T(1,128)S(1)}, s32[1,4]{1,0:T(1,128)}, u32[]{:S(2)}) copy-start(s32[1,4]{1,0:T(1,128)} %param.8) | copy-start | bytes 52
  233.0 40.5 %all-to-all-start = ((bf16[16,256,288]{1,2,0:T(8,128)(2,1)}), bf16[16,256,288]{1,2,0:T(8,128)(2,1)S(1)}, u32[]{:S(2)}, u32[]{:S(2)}) async-start(bf16[16,256,288]{1,2,0:T(8,128)(2,1)} %bitcast.85), calls=%async_computation | async-start | bytes 4718592 | tf_op jit(solution)/shard_map/all_to_all | solution.py:49
  238.2 111.5 %all-gather.7.cloned.1.call-start = ((), (), s32[]{:S(2)}) async-start(), calls=%async_computation.2 | async-start | bytes 8912896 | tf_op jit(solution)/shard_map/all_gather | solution.py:106
  274.5 1.4 copy-start
  366.6 8.4 %copy-start.1 = (f32[4,7,256,128]{3,2,1,0:T(8,128)S(1)}, f32[4,7,256,128]{3,2,1,0:T(8,128)}, u32[]{:S(2)}) copy-start(f32[4,7,256,128]{3,2,1,0:T(8,128)} %get-tuple-element.253) | copy-start | bytes 11010052 | tf_op jit(solution)/shard_map/while
  383.0 1.9 copy-start.2
  394.4 8.4 %copy-start.1 = (f32[4,7,256,128]{3,2,1,0:T(8,128)S(1)}, f32[4,7,256,128]{3,2,1,0:T(8,128)}, u32[]{:S(2)}) copy-start(f32[4,7,256,128]{3,2,1,0:T(8,128)} %get-tuple-element.253) | copy-start | bytes 11010052 | tf_op jit(solution)/shard_map/while
  410.8 1.9 copy-start.2
  422.1 8.4 %copy-start.1 = (f32[4,7,256,128]{3,2,1,0:T(8,128)S(1)}, f32[4,7,256,128]{3,2,1,0:T(8,128)}, u32[]{:S(2)}) copy-start(f32[4,7,256,128]{3,2,1,0:T(8,128)} %get-tuple-element.253) | copy-start | bytes 11010052 | tf_op jit(solution)/shard_map/while
  438.5 1.9 copy-start.2
  449.9 8.4 %copy-start.1 = (f32[4,7,256,128]{3,2,1,0:T(8,128)S(1)}, f32[4,7,256,128]{3,2,1,0:T(8,128)}, u32[]{:S(2)}) copy-start(f32[4,7,256,128]{3,2,1,0:T(8,128)} %get-tuple-element.253) | copy-start | bytes 11010052 | tf_op jit(solution)/shard_map/while
  466.3 1.9 copy-start.2
  477.6 8.4 %copy-start.1 = (f32[4,7,256,128]{3,2,1,0:T(8,128)S(1)}, f32[4,7,256,128]{3,2,1,0:T(8,128)}, u32[]{:S(2)}) copy-start(f32[4,7,256,128]{3,2,1,0:T(8,128)} %get-tuple-element.253) | copy-start | bytes 11010052 | tf_op jit(solution)/shard_map/while
  494.0 1.9 copy-start.2
  505.4 8.4 %copy-start.1 = (f32[4,7,256,128]{3,2,1,0:T(8,128)S(1)}, f32[4,7,256,128]{3,2,1,0:T(8,128)}, u32[]{:S(2)}) copy-start(f32[4,7,256,128]{3,2,1,0:T(8,128)} %get-tuple-element.253) | copy-start | bytes 11010052 | tf_op jit(solution)/shard_map/while
  521.8 1.9 copy-start.2
  533.1 8.4 %copy-start.1 = (f32[4,7,256,128]{3,2,1,0:T(8,128)S(1)}, f32[4,7,256,128]{3,2,1,0:T(8,128)}, u32[]{:S(2)}) copy-start(f32[4,7,256,128]{3,2,1,0:T(8,128)} %get-tuple-element.253) | copy-start | bytes 11010052 | tf_op jit(solution)/shard_map/while
  549.5 1.9 copy-start.2
  560.9 8.4 %copy-start.1 = (f32[4,7,256,128]{3,2,1,0:T(8,128)S(1)}, f32[4,7,256,128]{3,2,1,0:T(8,128)}, u32[]{:S(2)}) copy-start(f32[4,7,256,128]{3,2,1,0:T(8,128)} %get-tuple-element.253) | copy-start | bytes 11010052 | tf_op jit(solution)/shard_map/while
  577.3 1.9 copy-start.2
Sparse Core Ops, SparseCore 0:
  9.7 28.2 all-gather.8
  40.7 175.8 all-gather.4
  274.6 75.0 all-gather.6
where the time goes:
time: 597 us; the launch traced here: 595 us
  waiting for transfers between devices  297 us (50%)
  matrix products  131 us (22%)
  other arithmetic  87.5 us (15%)
  local copies, waits for them, and re-layouts  59.6 us (10%)
  between operations  13.9 us (2%)
    all_gather x1, waiting for transfers between devices, project_joined(): grouped = lax.all_gather(normed, 'gy', axis=0, tiled=True)  172 us
    reduce_sum x8, other arithmetic, attend(): total = total * shrink + jnp.sum(weights, axis=3)  66.5 us
    all_gather x1, waiting for transfers between devices, on_device(): piece = lax.all_gather(kv_rows, 'gy', axis=0, tiled=True)  65.9 us
    dot_general x8, matrix products, attend(): jnp.einsum('ghrn,ngo->ghro', weights.astype(jnp.bfloat16), value_part, pr...  64.3 us
    dot_general x8, matrix products, attend(): jnp.einsum('rgho,ngo->ghrn', queries, key_part, preferred_element_type=jn...  52.3 us
    all_to_all x1, waiting for transfers between devices, project_joined(): lax.all_to_all(block_out, 'gy', split_axis=0, concat_axis=1, tiled=True)  34.4 us
    all_gather x1, waiting for transfers between devices, project_joined(): lax.all_gather(weight, 'gx', axis=0, tiled=True)  24 us
    while x40, local copies, waits for them, and re-layouts  15 us
  transfers between devices with their start and end apart: 4, of which 4 were waited for; matrix products, arithmetic and copies ran while one was open for 4% of the time, Pallas kernels for 0%

commit v1 on v0

--- a/solution.py
+++ b/solution.py
@@ -46,7 +46,10 @@
     width = weight.shape[1]
     bias_block = lax.dynamic_slice_in_dim(bias, lax.axis_index("gy") * width, width, 0)
     block_out = (summed + bias_block[None, :]).astype(jnp.bfloat16)
-    return lax.all_to_all(block_out, "gy", split_axis=0, concat_axis=1, tiled=True)
+    return jnp.concatenate(
+        lax.all_to_all(jnp.stack(jnp.split(block_out, lax.axis_size("gy"), axis=0)), "gy", 0, 0),
+        axis=1,
+    )
 
 
 def on_device(hidden_in, lengths, attn_norm, qkv_weight, qkv_bias):

time: 597 us -> 613 us (1.027)
  local copies, waits for them, and re-layouts: 59.6 us -> 83.3 us
  waiting for transfers between devices: 297 us -> 286 us
    unnamed x8 -> x29, local copies, waits for them, and re-layouts: 10.1 us -> 24.9 us
    dynamic_slice x8 -> x24, local copies, waits for them, and re-layouts: 4.66 us -> 19.4 us  [on_device(): final_state, unused = lax.scan(advance, start_state, (stacked, offsets))]
    all_gather x1, waiting for transfers between devices: 65.9 us -> 54.2 us  [on_device(): piece = lax.all_gather(kv_rows, 'gy', axis=0, tiled=True)]
    while x40 -> x56, local copies, waits for them, and re-layouts: 15 us -> 26.2 us
    squeeze x8 -> x0, local copies, waits for them, and re-layouts: 10.4 us -> none  [on_device(): final_state, unused = lax.scan(advance, start_state, (stacked, offsets))]
    reshape x1 -> x0, local copies, waits for them, and re-layouts: 7.45 us -> none  [on_device(): stacked = piece.reshape(length // span, span, piece.shape[1])]
  transfers between devices with their start and end apart: 4 -> 4, of which waited for: 4 -> 4; matrix products, arithmetic and copies ran while one was open for 4% -> 5% of each run, Pallas kernels for 0% -> 0%
where the time goes in v1:
time: 613 us; the launch traced here: 611 us
  waiting for transfers between devices  286 us (47%)
  matrix products  131 us (21%)
  other arithmetic  91 us (15%)
  local copies, waits for them, and re-layouts  83.3 us (14%)
  between operations  13.9 us (2%)
    all_gather x1, waiting for transfers between devices, project_joined(): grouped = lax.all_gather(normed, 'gy', axis=0, tiled=True)  172 us
    reduce_sum x8, other arithmetic, attend(): total = total * shrink + jnp.sum(weights, axis=3)  66.5 us
    dot_general x8, matrix products, attend(): jnp.einsum('ghrn,ngo->ghro', weights.astype(jnp.bfloat16), value_part, pr...  64.3 us
    all_gather x1, waiting for transfers between devices, on_device(): piece = lax.all_gather(kv_rows, 'gy', axis=0, tiled=True)  54.2 us
    dot_general x8, matrix products, attend(): jnp.einsum('rgho,ngo->ghrn', queries, key_part, preferred_element_type=jn...  52.1 us
    all_to_all x1, waiting for transfers between devices, project_joined(): lax.all_to_all(jnp.stack(jnp.split(block_out, lax.axis_size('gy'), axis=0...  33.7 us
    while x56, local copies, waits for them, and re-layouts  26.2 us
    unnamed x29, local copies, waits for them, and re-layouts  24.9 us
  transfers between devices with their start and end apart: 4, of which 4 were waited for; matrix products, arithmetic and copies ran while one was open for 5% of the time, Pallas kernels for 0%

profile of v1, /device:TPU:0, one launch (start us, length us, event | category | flops | bytes accessed | tf_op | source)
XLA Modules:
  0.0 610.9 jit_solution(10762567063647683288)
XLA Ops:
  13.2 24.8 %all-gather.9.cloned.1.call-done = bf16[8,448,288]{1,2,0:T(8,128)(2,1)} async-done(((bf16[1,448,288]{1,2,0:T(8,128)(2,1)}), bf16[8,448,288]{1,2,0:T(8,128)(2,1)}) %all-gather.9.cloned.1.call-update) | async-done | bytes 2064400 | tf_op jit(solution)/shard_map/all_gather | solution.py:43
  44.5 172.1 %all-gather.5.cloned.1.call-done = bf16[4096,3584]{1,0:T(8,128)(2,1)} async-done(((bf16[256,3584]{1,0:T(8,128)(2,1)}), bf16[4096,3584]{1,0:T(8,128)(2,1)}) %all-gather.5.cloned.1.call-update) | async-done | bytes 29360144 | tf_op jit(solution)/shard_map/all_gather | solution.py:40
  216.6 14.7 %fusion.16 = bf16[4096,288]{0,1:T(8,128)(2,1)S(1)} fusion(bf16[4096,3584]{1,0:T(8,128)(2,1)} %all-gather.5.cloned.1.call-done, bf16[3584,288]{0,1:T(8,128)(2,1)} %reshape.177, f32[288]{0:T(512)S(1)} %dynamic_slice.11), kind=kOutput, calls=%fused_computation.24 | convolution fusion | flops 8458076160 | bytes 33784960 | tf_op jit(solution)/shard_map/dot_general | solution.py:41
  242.1 5.4 all-to-all-start
  249.1 33.7 %all-to-all-done = bf16[16,256,288]{1,2,0:T(8,128)(2,1)S(1)} async-done(((bf16[16,256,288]{1,2,0:T(8,128)(2,1)}), bf16[16,256,288]{1,2,0:T(8,128)(2,1)S(1)}, u32[]{:S(2)}, u32[]{:S(2)}) %all-to-all-start) | async-done | bytes 2359328 | tf_op jit(solution)/shard_map/all_to_all | solution.py:50
  303.8 54.2 %all-gather.7.cloned.1.call-done = bf16[4096,1024]{1,0:T(8,128)(2,1)} async-done(((bf16[256,1024]{1,0:T(8,128)(2,1)}), bf16[4096,1024]{1,0:T(8,128)(2,1)}) %all-gather.7.cloned.1.call-update) | async-done | bytes 8388624 | tf_op jit(solution)/shard_map/all_gather | solution.py:109
  358.1 236.7 %while.15 = (s32[]{:T(128)}, f32[4,7,256]{2,1,0:T(8,128)S(1)}, f32[4,7,256]{2,1,0:T(8,128)S(1)}, f32[4,7,256,128]{3,2,1,0:T(8,128)}, s32[256]{0:T(256)S(1)}, /*i...) while((s32[]{:T(128)}, f32[4,7,256]{2,1,0:T(8,128)S(1)}, ...), condition=%wide.region_8.9_spmd.clone, body=%wide.region_4.8_spmd.clone.sunk | while | flops 1922606336 | bytes 98252016 | solution.py:118
  362.9 6.5 %fusion.61 = (f32[4,7,256]{2,1,0:T(8,128)S(1)}, f32[4,512,256,7]{2,1,3,0:T(8,128)}) fusion(pred[256,512]{0,1:T(8,128)(4,1)S(1)} %compare_and_fusion.2, bf16[512,4,128,1]{0,2,3,1:T(8,128)(2,1)S(1)} %bitcast.141, bf16[256,4,7,128]{3,0,2,1:T(8,128)(2,1)S(1)} %copy-done), kind=kOutput, calls=%fused_computation.3.clone.1 | convolution fusion | flops 950526976 | bytes 17199104 | tf_op jit(solution)/shard_map/while/body/eval_jaxpr/rgho,ngo->ghrn/dot_general | solution.py:83
  369.4 8.3 %fusion.62 = f32[4,7,256]{2,1,0:T(8,128)S(1)} fusion(f32[4,512,256,7]{2,1,3,0:T(8,128)} %get-tuple-element.238, f32[4,7,256]{2,1,0:T(8,128)S(1)} %select_maximum_fusion.2, pred[256,512]{0,1:T(8,128)(4,1)S(1)} %compare_and_fusion.2), kind=kLoop, calls=%fused_computation.7.clone.1 | loop fusion | flops 14672896 | bytes 14868480 | tf_op jit(solution)/shard_map/while/body/eval_jaxpr/reduce_sum | solution.py:92
  377.7 8.0 %fusion.64 = f32[4,7,256,128]{3,2,1,0:T(8,128)S(1)} fusion(f32[4,7,256,128]{3,2,1,0:T(8,128)S(1)} %copy-done.2, bf16[512,4,128,1]{0,2,3,1:T(8,128)(2,1)S(1)} %bitcast.143, f32[4,512,256,7]{2,1,3,0:T(8,128)} %get-tuple-element.238, f32[4,7,256]{2,1,0:T(8,128)S(1)} %select_maximum_fusion.2, pred[256,512]{0,1:T(8,128)(4,1)S(1)} %compare_and_fusion.2, ...), kind=kOutput, calls=%fused_computation.11.clone.1 | convolution fusion | flops 956956672 | bytes 22732800 | tf_op jit(solution)/shard_map/while/body/eval_jaxpr/ghrn,ngo->ghro/dot_general | solution.py:93
  392.4 6.5 %fusion.61 = (f32[4,7,256]{2,1,0:T(8,128)S(1)}, f32[4,512,256,7]{2,1,3,0:T(8,128)}) fusion(pred[256,512]{0,1:T(8,128)(4,1)S(1)} %compare_and_fusion.2, bf16[512,4,128,1]{0,2,3,1:T(8,128)(2,1)S(1)} %bitcast.141, bf16[256,4,7,128]{3,0,2,1:T(8,128)(2,1)S(1)} %copy-done), kind=kOutput, calls=%fused_computation.3.clone.1 | convolution fusion | flops 950526976 | bytes 17199104 | tf_op jit(solution)/shard_map/while/body/eval_jaxpr/rgho,ngo->ghrn/dot_general | solution.py:83
  399.0 8.3 %fusion.62 = f32[4,7,256]{2,1,0:T(8,128)S(1)} fusion(f32[4,512,256,7]{2,1,3,0:T(8,128)} %get-tuple-element.238, f32[4,7,256]{2,1,0:T(8,128)S(1)} %select_maximum_fusion.2, pred[256,512]{0,1:T(8,128)(4,1)S(1)} %compare_and_fusion.2), kind=kLoop, calls=%fused_computation.7.clone.1 | loop fusion | flops 14672896 | bytes 14868480 | tf_op jit(solution)/shard_map/while/body/eval_jaxpr/reduce_sum | solution.py:92
  407.3 8.0 %fusion.64 = f32[4,7,256,128]{3,2,1,0:T(8,128)S(1)} fusion(f32[4,7,256,128]{3,2,1,0:T(8,128)S(1)} %copy-done.2, bf16[512,4,128,1]{0,2,3,1:T(8,128)(2,1)S(1)} %bitcast.143, f32[4,512,256,7]{2,1,3,0:T(8,128)} %get-tuple-element.238, f32[4,7,256]{2,1,0:T(8,128)S(1)} %select_maximum_fusion.2, pred[256,512]{0,1:T(8,128)(4,1)S(1)} %compare_and_fusion.2, ...), kind=kOutput, calls=%fused_computation.11.clone.1 | convolution fusion | flops 956956672 | bytes 22732800 | tf_op jit(solution)/shard_map/while/body/eval_jaxpr/ghrn,ngo->ghro/dot_general | solution.py:93
  422.0 6.5 %fusion.61 = (f32[4,7,256]{2,1,0:T(8,128)S(1)}, f32[4,512,256,7]{2,1,3,0:T(8,128)}) fusion(pred[256,512]{0,1:T(8,128)(4,1)S(1)} %compare_and_fusion.2, bf16[512,4,128,1]{0,2,3,1:T(8,128)(2,1)S(1)} %bitcast.141, bf16[256,4,7,128]{3,0,2,1:T(8,128)(2,1)S(1)} %copy-done), kind=kOutput, calls=%fused_computation.3.clone.1 | convolution fusion | flops 950526976 | bytes 17199104 | tf_op jit(solution)/shard_map/while/body/eval_jaxpr/rgho,ngo->ghrn/dot_general | solution.py:83
  428.5 8.3 %fusion.62 = f32[4,7,256]{2,1,0:T(8,128)S(1)} fusion(f32[4,512,256,7]{2,1,3,0:T(8,128)} %get-tuple-element.238, f32[4,7,256]{2,1,0:T(8,128)S(1)} %select_maximum_fusion.2, pred[256,512]{0,1:T(8,128)(4,1)S(1)} %compare_and_fusion.2), kind=kLoop, calls=%fused_computation.7.clone.1 | loop fusion | flops 14672896 | bytes 14868480 | tf_op jit(solution)/shard_map/while/body/eval_jaxpr/reduce_sum | solution.py:92
  436.9 8.0 %fusion.64 = f32[4,7,256,128]{3,2,1,0:T(8,128)S(1)} fusion(f32[4,7,256,128]{3,2,1,0:T(8,128)S(1)} %copy-done.2, bf16[512,4,128,1]{0,2,3,1:T(8,128)(2,1)S(1)} %bitcast.143, f32[4,512,256,7]{2,1,3,0:T(8,128)} %get-tuple-element.238, f32[4,7,256]{2,1,0:T(8,128)S(1)} %select_maximum_fusion.2, pred[256,512]{0,1:T(8,128)(4,1)S(1)} %compare_and_fusion.2, ...), kind=kOutput, calls=%fused_computation.11.clone.1 | convolution fusion | flops 956956672 | bytes 22732800 | tf_op jit(solution)/shard_map/while/body/eval_jaxpr/ghrn,ngo->ghro/dot_general | solution.py:93
  451.6 6.5 %fusion.61 = (f32[4,7,256]{2,1,0:T(8,128)S(1)}, f32[4,512,256,7]{2,1,3,0:T(8,128)}) fusion(pred[256,512]{0,1:T(8,128)(4,1)S(1)} %compare_and_fusion.2, bf16[512,4,128,1]{0,2,3,1:T(8,128)(2,1)S(1)} %bitcast.141, bf16[256,4,7,128]{3,0,2,1:T(8,128)(2,1)S(1)} %copy-done), kind=kOutput, calls=%fused_computation.3.clone.1 | convolution fusion | flops 950526976 | bytes 17199104 | tf_op jit(solution)/shard_map/while/body/eval_jaxpr/rgho,ngo->ghrn/dot_general | solution.py:83
  458.1 8.3 %fusion.62 = f32[4,7,256]{2,1,0:T(8,128)S(1)} fusion(f32[4,512,256,7]{2,1,3,0:T(8,128)} %get-tuple-element.238, f32[4,7,256]{2,1,0:T(8,128)S(1)} %select_maximum_fusion.2, pred[256,512]{0,1:T(8,128)(4,1)S(1)} %compare_and_fusion.2), kind=kLoop, calls=%fused_computation.7.clone.1 | loop fusion | flops 14672896 | bytes 14868480 | tf_op jit(solution)/shard_map/while/body/eval_jaxpr/reduce_sum | solution.py:92
  466.5 8.0 %fusion.64 = f32[4,7,256,128]{3,2,1,0:T(8,128)S(1)} fusion(f32[4,7,256,128]{3,2,1,0:T(8,128)S(1)} %copy-done.2, bf16[512,4,128,1]{0,2,3,1:T(8,128)(2,1)S(1)} %bitcast.143, f32[4,512,256,7]{2,1,3,0:T(8,128)} %get-tuple-element.238, f32[4,7,256]{2,1,0:T(8,128)S(1)} %select_maximum_fusion.2, pred[256,512]{0,1:T(8,128)(4,1)S(1)} %compare_and_fusion.2, ...), kind=kOutput, calls=%fused_computation.11.clone.1 | convolution fusion | flops 956956672 | bytes 22732800 | tf_op jit(solution)/shard_map/while/body/eval_jaxpr/ghrn,ngo->ghro/dot_general | solution.py:93
  481.2 6.5 %fusion.61 = (f32[4,7,256]{2,1,0:T(8,128)S(1)}, f32[4,512,256,7]{2,1,3,0:T(8,128)}) fusion(pred[256,512]{0,1:T(8,128)(4,1)S(1)} %compare_and_fusion.2, bf16[512,4,128,1]{0,2,3,1:T(8,128)(2,1)S(1)} %bitcast.141, bf16[256,4,7,128]{3,0,2,1:T(8,128)(2,1)S(1)} %copy-done), kind=kOutput, calls=%fused_computation.3.clone.1 | convolution fusion | flops 950526976 | bytes 17199104 | tf_op jit(solution)/shard_map/while/body/eval_jaxpr/rgho,ngo->ghrn/dot_general | solution.py:83
  487.7 8.3 %fusion.62 = f32[4,7,256]{2,1,0:T(8,128)S(1)} fusion(f32[4,512,256,7]{2,1,3,0:T(8,128)} %get-tuple-element.238, f32[4,7,256]{2,1,0:T(8,128)S(1)} %select_maximum_fusion.2, pred[256,512]{0,1:T(8,128)(4,1)S(1)} %compare_and_fusion.2), kind=kLoop, calls=%fused_computation.7.clone.1 | loop fusion | flops 14672896 | bytes 14868480 | tf_op jit(solution)/shard_map/while/body/eval_jaxpr/reduce_sum | solution.py:92
  496.1 8.0 %fusion.64 = f32[4,7,256,128]{3,2,1,0:T(8,128)S(1)} fusion(f32[4,7,256,128]{3,2,1,0:T(8,128)S(1)} %copy-done.2, bf16[512,4,128,1]{0,2,3,1:T(8,128)(2,1)S(1)} %bitcast.143, f32[4,512,256,7]{2,1,3,0:T(8,128)} %get-tuple-element.238, f32[4,7,256]{2,1,0:T(8,128)S(1)} %select_maximum_fusion.2, pred[256,512]{0,1:T(8,128)(4,1)S(1)} %compare_and_fusion.2, ...), kind=kOutput, calls=%fused_computation.11.clone.1 | convolution fusion | flops 956956672 | bytes 22732800 | tf_op jit(solution)/shard_map/while/body/eval_jaxpr/ghrn,ngo->ghro/dot_general | solution.py:93
  510.8 6.5 %fusion.61 = (f32[4,7,256]{2,1,0:T(8,128)S(1)}, f32[4,512,256,7]{2,1,3,0:T(8,128)}) fusion(pred[256,512]{0,1:T(8,128)(4,1)S(1)} %compare_and_fusion.2, bf16[512,4,128,1]{0,2,3,1:T(8,128)(2,1)S(1)} %bitcast.141, bf16[256,4,7,128]{3,0,2,1:T(8,128)(2,1)S(1)} %copy-done), kind=kOutput, calls=%fused_computation.3.clone.1 | convolution fusion | flops 950526976 | bytes 17199104 | tf_op jit(solution)/shard_map/while/body/eval_jaxpr/rgho,ngo->ghrn/dot_general | solution.py:83
  517.3 8.3 %fusion.62 = f32[4,7,256]{2,1,0:T(8,128)S(1)} fusion(f32[4,512,256,7]{2,1,3,0:T(8,128)} %get-tuple-element.238, f32[4,7,256]{2,1,0:T(8,128)S(1)} %select_maximum_fusion.2, pred[256,512]{0,1:T(8,128)(4,1)S(1)} %compare_and_fusion.2), kind=kLoop, calls=%fused_computation.7.clone.1 | loop fusion | flops 14672896 | bytes 14868480 | tf_op jit(solution)/shard_map/while/body/eval_jaxpr/reduce_sum | solution.py:92
  525.6 8.0 %fusion.64 = f32[4,7,256,128]{3,2,1,0:T(8,128)S(1)} fusion(f32[4,7,256,128]{3,2,1,0:T(8,128)S(1)} %copy-done.2, bf16[512,4,128,1]{0,2,3,1:T(8,128)(2,1)S(1)} %bitcast.143, f32[4,512,256,7]{2,1,3,0:T(8,128)} %get-tuple-element.238, f32[4,7,256]{2,1,0:T(8,128)S(1)} %select_maximum_fusion.2, pred[256,512]{0,1:T(8,128)(4,1)S(1)} %compare_and_fusion.2, ...), kind=kOutput, calls=%fused_computation.11.clone.1 | convolution fusion | flops 956956672 | bytes 22732800 | tf_op jit(solution)/shard_map/while/body/eval_jaxpr/ghrn,ngo->ghro/dot_general | solution.py:93
  540.4 6.5 %fusion.61 = (f32[4,7,256]{2,1,0:T(8,128)S(1)}, f32[4,512,256,7]{2,1,3,0:T(8,128)}) fusion(pred[256,512]{0,1:T(8,128)(4,1)S(1)} %compare_and_fusion.2, bf16[512,4,128,1]{0,2,3,1:T(8,128)(2,1)S(1)} %bitcast.141, bf16[256,4,7,128]{3,0,2,1:T(8,128)(2,1)S(1)} %copy-done), kind=kOutput, calls=%fused_computation.3.clone.1 | convolution fusion | flops 950526976 | bytes 17199104 | tf_op jit(solution)/shard_map/while/body/eval_jaxpr/rgho,ngo->ghrn/dot_general | solution.py:83
  546.9 8.3 %fusion.62 = f32[4,7,256]{2,1,0:T(8,128)S(1)} fusion(f32[4,512,256,7]{2,1,3,0:T(8,128)} %get-tuple-element.238, f32[4,7,256]{2,1,0:T(8,128)S(1)} %select_maximum_fusion.2, pred[256,512]{0,1:T(8,128)(4,1)S(1)} %compare_and_fusion.2), kind=kLoop, calls=%fused_computation.7.clone.1 | loop fusion | flops 14672896 | bytes 14868480 | tf_op jit(solution)/shard_map/while/body/eval_jaxpr/reduce_sum | solution.py:92
  555.2 8.0 %fusion.64 = f32[4,7,256,128]{3,2,1,0:T(8,128)S(1)} fusion(f32[4,7,256,128]{3,2,1,0:T(8,128)S(1)} %copy-done.2, bf16[512,4,128,1]{0,2,3,1:T(8,128)(2,1)S(1)} %bitcast.143, f32[4,512,256,7]{2,1,3,0:T(8,128)} %get-tuple-element.238, f32[4,7,256]{2,1,0:T(8,128)S(1)} %select_maximum_fusion.2, pred[256,512]{0,1:T(8,128)(4,1)S(1)} %compare_and_fusion.2, ...), kind=kOutput, calls=%fused_computation.11.clone.1 | convolution fusion | flops 956956672 | bytes 22732800 | tf_op jit(solution)/shard_map/while/body/eval_jaxpr/ghrn,ngo->ghro/dot_general | solution.py:93
  569.9 6.5 %fusion.61 = (f32[4,7,256]{2,1,0:T(8,128)S(1)}, f32[4,512,256,7]{2,1,3,0:T(8,128)}) fusion(pred[256,512]{0,1:T(8,128)(4,1)S(1)} %compare_and_fusion.2, bf16[512,4,128,1]{0,2,3,1:T(8,128)(2,1)S(1)} %bitcast.141, bf16[256,4,7,128]{3,0,2,1:T(8,128)(2,1)S(1)} %copy-done), kind=kOutput, calls=%fused_computation.3.clone.1 | convolution fusion | flops 950526976 | bytes 17199104 | tf_op jit(solution)/shard_map/while/body/eval_jaxpr/rgho,ngo->ghrn/dot_general | solution.py:83
  576.5 8.3 %fusion.62 = f32[4,7,256]{2,1,0:T(8,128)S(1)} fusion(f32[4,512,256,7]{2,1,3,0:T(8,128)} %get-tuple-element.238, f32[4,7,256]{2,1,0:T(8,128)S(1)} %select_maximum_fusion.2, pred[256,512]{0,1:T(8,128)(4,1)S(1)} %compare_and_fusion.2), kind=kLoop, calls=%fused_computation.7.clone.1 | loop fusion | flops 14672896 | bytes 14868480 | tf_op jit(solution)/shard_map/while/body/eval_jaxpr/reduce_sum | solution.py:92
  584.8 8.0 %fusion.64 = f32[4,7,256,128]{3,2,1,0:T(8,128)S(1)} fusion(f32[4,7,256,128]{3,2,1,0:T(8,128)S(1)} %copy-done.2, bf16[512,4,128,1]{0,2,3,1:T(8,128)(2,1)S(1)} %bitcast.143, f32[4,512,256,7]{2,1,3,0:T(8,128)} %get-tuple-element.238, f32[4,7,256]{2,1,0:T(8,128)S(1)} %select_maximum_fusion.2, pred[256,512]{0,1:T(8,128)(4,1)S(1)} %compare_and_fusion.2, ...), kind=kOutput, calls=%fused_computation.11.clone.1 | convolution fusion | flops 956956672 | bytes 22732800 | tf_op jit(solution)/shard_map/while/body/eval_jaxpr/ghrn,ngo->ghro/dot_general | solution.py:93
  594.7 4.6 copy.48
  (197 shorter events, 104.1 us)
Async XLA Ops:
  7.2 2.7 copy-start.1
  7.2 30.8 %all-gather.9.cloned.1.call-start = ((), (), s32[]{:S(2)}) async-start(), calls=%async_computation.3 | async-start | bytes 2654208 | tf_op jit(solution)/shard_map/all_gather | solution.py:43
  7.9 208.7 %all-gather.5.cloned.1.call-start = ((), (), s32[]{:S(2)}) async-start(), calls=%async_computation.1 | async-start | bytes 31195136 | tf_op jit(solution)/shard_map/all_gather | solution.py:40
  242.1 5.5 copy-start.5
  242.1 40.6 %all-to-all-start = ((bf16[16,256,288]{1,2,0:T(8,128)(2,1)}), bf16[16,256,288]{1,2,0:T(8,128)(2,1)S(1)}, u32[]{:S(2)}, u32[]{:S(2)}) async-start(bf16[16,256,288]{1,2,0:T(8,128)(2,1)} %fusion.20), calls=%async_computation | async-start | bytes 4718592 | tf_op jit(solution)/shard_map/all_to_all | solution.py:50
  247.5 110.5 %all-gather.7.cloned.1.call-start = ((), (), s32[]{:S(2)}) async-start(), calls=%async_computation.2 | async-start | bytes 8912896 | tf_op jit(solution)/shard_map/all_gather | solution.py:109
  294.6 2.5 copy-start.4
  361.4 1.5 copy-start
  369.4 8.4 %copy-start.2 = (f32[4,7,256,128]{3,2,1,0:T(8,128)S(1)}, f32[4,7,256,128]{3,2,1,0:T(8,128)}, u32[]{:S(2)}) copy-start(f32[4,7,256,128]{3,2,1,0:T(8,128)} %get-tuple-element.257) | copy-start | bytes 11010052 | tf_op jit(solution)/shard_map/while
  385.8 1.9 copy-start.3
  390.9 1.5 copy-start
  399.0 8.4 %copy-start.2 = (f32[4,7,256,128]{3,2,1,0:T(8,128)S(1)}, f32[4,7,256,128]{3,2,1,0:T(8,128)}, u32[]{:S(2)}) copy-start(f32[4,7,256,128]{3,2,1,0:T(8,128)} %get-tuple-element.257) | copy-start | bytes 11010052 | tf_op jit(solution)/shard_map/while
  415.4 1.9 copy-start.3
  420.5 1.5 copy-start
  428.5 8.4 %copy-start.2 = (f32[4,7,256,128]{3,2,1,0:T(8,128)S(1)}, f32[4,7,256,128]{3,2,1,0:T(8,128)}, u32[]{:S(2)}) copy-start(f32[4,7,256,128]{3,2,1,0:T(8,128)} %get-tuple-element.257) | copy-start | bytes 11010052 | tf_op jit(solution)/shard_map/while
  444.9 1.9 copy-start.3
  450.1 1.5 copy-start
  458.1 8.4 %copy-start.2 = (f32[4,7,256,128]{3,2,1,0:T(8,128)S(1)}, f32[4,7,256,128]{3,2,1,0:T(8,128)}, u32[]{:S(2)}) copy-start(f32[4,7,256,128]{3,2,1,0:T(8,128)} %get-tuple-element.257) | copy-start | bytes 11010052 | tf_op jit(solution)/shard_map/while
  474.5 1.9 copy-start.3
  479.7 1.5 copy-start
  487.7 8.4 %copy-start.2 = (f32[4,7,256,128]{3,2,1,0:T(8,128)S(1)}, f32[4,7,256,128]{3,2,1,0:T(8,128)}, u32[]{:S(2)}) copy-start(f32[4,7,256,128]{3,2,1,0:T(8,128)} %get-tuple-element.257) | copy-start | bytes 11010052 | tf_op jit(solution)/shard_map/while
  504.1 1.9 copy-start.3
  509.3 1.5 copy-start
  517.3 8.4 %copy-start.2 = (f32[4,7,256,128]{3,2,1,0:T(8,128)S(1)}, f32[4,7,256,128]{3,2,1,0:T(8,128)}, u32[]{:S(2)}) copy-start(f32[4,7,256,128]{3,2,1,0:T(8,128)} %get-tuple-element.257) | copy-start | bytes 11010052 | tf_op jit(solution)/shard_map/while
  533.7 1.9 copy-start.3
  538.9 1.5 copy-start
  546.9 8.4 %copy-start.2 = (f32[4,7,256,128]{3,2,1,0:T(8,128)S(1)}, f32[4,7,256,128]{3,2,1,0:T(8,128)}, u32[]{:S(2)}) copy-start(f32[4,7,256,128]{3,2,1,0:T(8,128)} %get-tuple-element.257) | copy-start | bytes 11010052 | tf_op jit(solution)/shard_map/while
  563.3 1.9 copy-start.3
  568.4 1.5 copy-start
  576.5 8.4 %copy-start.2 = (f32[4,7,256,128]{3,2,1,0:T(8,128)S(1)}, f32[4,7,256,128]{3,2,1,0:T(8,128)}, u32[]{:S(2)}) copy-start(f32[4,7,256,128]{3,2,1,0:T(8,128)} %get-tuple-element.257) | copy-start | bytes 11010052 | tf_op jit(solution)/shard_map/while
  592.9 1.9 copy-start.3
Sparse Core Ops, SparseCore 0:
  9.7 28.2 all-gather.8
  40.7 175.8 all-gather.4
  289.4 68.6 all-gather.6
